TPU v7x, 32 devices: a whole 2x2x4 slice. The times are simulated.
32 devices in a mesh: dp: 8 (over z, core), leaf: 4 (over y, x).
Axes of the slice: x: 2, y: 2, z: 4, core: 2. Of those that a mesh axis runs over, the one named last changes fastest.
Arguments:
- features: bfloat16 [51200, 384], P(('dp', 'leaf')), may hold values from -6 to 6
- head_weight: bfloat16 [384, 1536], replicated, may hold values from -0.3125 to 0.3125
- gain: float32 [1536], replicated, may hold values from 0.5 to 1.5
- shift: float32 [1536], replicated, may hold values from -3 to 3
- node_weights: bfloat16 [4096, 1536], P('leaf'), may hold values from -0.15625 to 0.15625
- subtree_map: int32 [64], replicated, may hold values from 0 to 63, each once
- node_ids: int32 [512, 64], P('dp'), may hold values from -1 to 4095, as said below
Outputs:
- head_grad: float32 [384, 1536], P(None, 'dp')
- gain_grad: float32 [1536], P('dp')
- shift_grad: float32 [1536], P('dp')
- node_grad: float32 [4096, 1536], P('leaf', 'dp')
Inputs may be any that keep to these rules, and one draw needn't show every extreme that they name: `node_ids`: each image has 1 to 16 positive ids, all in one subtree, in its first columns, then -1; and 1 to 48 hard-negative ids in another subtree from column 16 on, then -1. Ids of one image are distinct. The first image has full counts.
All inputs are finite; a program needn't handle non-finite values.
Results may differ from a plain program's by a relative error of at most 0.0036.
Values may be sent and summed in bfloat16 or wider, within the bound.
No kernel may reach another device: no remote copies, remote signals or barrier semaphores. Data moves between devices by JAX's collectives and lax.ppermute only.
A program may use at most 128 MiB of HBM per device.

v0:
```python
import jax
import jax.numpy as jnp
from jax import lax
from jax.sharding import PartitionSpec as P

P_SIZE = 100
SUB_SIZE = 64
KPOS = 16
HIGHEST = lax.Precision.HIGHEST


def block_table(pos_vec, pos_blk, neg_vec, neg_blk, blocks):
    lane_block = jnp.arange(blocks * SUB_SIZE, dtype=jnp.int32)[None, :] // SUB_SIZE
    pos_wide = jnp.tile(pos_vec, (1, blocks))
    neg_wide = jnp.tile(neg_vec, (1, blocks))
    pos_part = jnp.where(lane_block == pos_blk[:, None], pos_wide, 0.0)
    neg_part = jnp.where(lane_block == neg_blk[:, None], neg_wide, 0.0)
    return pos_part + neg_part


def pick_block(values, blk, blocks):
    rows = values.shape[0]
    split = values.reshape(rows, blocks, SUB_SIZE)
    hit = jnp.arange(blocks, dtype=jnp.int32)[None, :, None] == blk[:, None, None]
    return jnp.sum(jnp.where(hit, split, 0.0), axis=1)


def lane_mask(ids, valid):
    column = jnp.arange(SUB_SIZE, dtype=jnp.int32)[None, None, :]
    hit = ((ids % SUB_SIZE)[:, :, None] == column) & valid[:, :, None]
    return jnp.any(hit, axis=1)


def shards(features, head_weight, gain, shift, node_weights, subtree_map, node_ids):
    rows = features.shape[0]
    images_here = rows // P_SIZE
    width = head_weight.shape[1]
    slots_dev = node_weights.shape[0]
    blocks = slots_dev // SUB_SIZE
    n_dp = lax.axis_size("dp")
    leaf = lax.axis_index("leaf")
    select = (
        jnp.arange(rows, dtype=jnp.int32)[None, :] // P_SIZE
        == jnp.arange(images_here, dtype=jnp.int32)[:, None]
    ).astype(jnp.float32)
    linear_scores = jnp.dot(features, head_weight, preferred_element_type=jnp.float32)
    shifted = gain * linear_scores + shift
    sig = jax.nn.sigmoid(shifted)
    active = shifted * sig
    image_sum = jnp.dot(select, active, precision=HIGHEST, preferred_element_type=jnp.float32)
    embedded = (image_sum / P_SIZE).astype(jnp.bfloat16)
    grouped = lax.all_gather(embedded, "leaf", axis=0, tiled=True)
    group = grouped.shape[0]
    valid = node_ids >= 0
    safe_ids = jnp.where(valid, node_ids, 0)
    block_of = subtree_map[safe_ids // SUB_SIZE]
    pos_block = block_of[:, 0]
    neg_block = block_of[:, KPOS]
    pos_here = jnp.where(pos_block // blocks == leaf, pos_block % blocks, -1)
    neg_here = jnp.where(neg_block // blocks == leaf, neg_block % blocks, -1)
    pos_mask = lane_mask(safe_ids[:, :KPOS], valid[:, :KPOS])
    neg_mask = lane_mask(safe_ids[:, KPOS:], valid[:, KPOS:])
    scores = lax.dot_general(
        grouped, node_weights, (((1,), (1,)), ((), ())), preferred_element_type=jnp.float32
    )
    pos_logit = pick_block(scores, pos_here, blocks)
    neg_logit = pick_block(scores, neg_here, blocks)
    pos_coef = jnp.where(pos_mask & (pos_here >= 0)[:, None], jax.nn.sigmoid(pos_logit) - 1.0, 0.0)
    neg_coef = jnp.where(neg_mask & (neg_here >= 0)[:, None], jax.nn.sigmoid(neg_logit), 0.0)
    pos_coef = pos_coef.astype(jnp.bfloat16)
    neg_coef = neg_coef.astype(jnp.bfloat16)
    table = block_table(pos_coef, pos_here, neg_coef, neg_here, blocks).astype(jnp.bfloat16)
    grad_part = jnp.dot(table, node_weights, preferred_element_type=jnp.float32)
    emb_grad = lax.psum_scatter(grad_part, "leaf", scatter_dimension=0, tiled=True)
    col_width = width // n_dp
    column_chunks = grouped.reshape(group, n_dp, col_width).transpose(1, 0, 2)
    compact = jnp.concatenate(
        [
            pos_coef,
            neg_coef,
            pos_here[:, None].astype(jnp.bfloat16),
            neg_here[:, None].astype(jnp.bfloat16),
        ],
        axis=1,
    )
    send = jnp.concatenate(
        [column_chunks, jnp.broadcast_to(compact[None], (n_dp,) + compact.shape)], axis=2
    )
    recv = lax.all_to_all(send, "dp", split_axis=0, concat_axis=0, tiled=True)
    columns = recv[:, :, :col_width].reshape(n_dp * group, col_width)
    info = recv[:, :, col_width:].reshape(n_dp * group, compact.shape[1])
    all_pos = info[:, :SUB_SIZE]
    all_neg = info[:, SUB_SIZE : 2 * SUB_SIZE]
    all_pos_blk = info[:, 2 * SUB_SIZE].astype(jnp.int32)
    all_neg_blk = info[:, 2 * SUB_SIZE + 1].astype(jnp.int32)
    all_table = block_table(all_pos, all_pos_blk, all_neg, all_neg_blk, blocks).astype(jnp.bfloat16)
    node_grad = lax.dot_general(
        all_table, columns, (((0,), (0,)), ((), ())), preferred_element_type=jnp.float32
    )
    spread = jnp.dot(
        select.T, emb_grad / P_SIZE, precision=HIGHEST, preferred_element_type=jnp.float32
    )
    pixel_gradient = spread * (sig * (1.0 + shifted * (1.0 - sig)))
    lin_grad = (pixel_gradient * gain).astype(jnp.bfloat16)
    head_term = lax.dot_general(
        features, lin_grad, (((0,), (0,)), ((), ())), preferred_element_type=jnp.float32
    )
    gain_term = jnp.sum(pixel_gradient * linear_scores, axis=0)
    shift_term = jnp.sum(pixel_gradient, axis=0)
    stacked = jnp.concatenate([head_term, gain_term[None], shift_term[None]], axis=0)
    reduced = lax.psum(lax.psum_scatter(stacked, "dp", scatter_dimension=1, tiled=True), "leaf")
    e_size = head_term.shape[0]
    return (reduced[:e_size], reduced[e_size], reduced[e_size + 1], node_grad)


def solution(mesh):
    in_specs = (P(("dp", "leaf"), None), P(), P(), P(), P("leaf", None), P(), P("dp", None))
    out_specs = (P(None, "dp"), P("dp"), P("dp"), P("leaf", "dp"))
    return jax.shard_map(shards, mesh=mesh, in_specs=in_specs, out_specs=out_specs, check_vma=False)
```

profile of v0, /device:TPU:0, one launch (start us, length us, event | category | flops | bytes accessed | tf_op | source)
XLA Modules:
  0.0 220.9 jit_solution(9904976137338489691)
XLA Ops:
  7.3 0.9 broadcast_select_fusion
  10.4 24.7 %gather_fusion = s32[4096]{0:T(1024)S(1)} fusion(s32[64]{0:T(128)S(1)} %copy-done.1, s32[4096]{0:T(1024)S(1)} %broadcast_clamp_fusion), kind=kCustom, calls=%fused_computation | custom fusion | bytes 49152 | tf_op jit(solution)/shard_map/gather | solution.py:56
  37.8 4.4 %fusion.58 = f32[1600,1536]{1,0:T(8,128)S(1)} fusion(bf16[1600,384]{1,0:T(8,128)(2,1)} %param.7, bf16[384,1536]{1,0:T(8,128)(2,1)} %param.8), kind=kOutput, calls=%fused_computation.131 | convolution fusion | flops 1887436800 | bytes 12238848 | tf_op jit(solution)/shard_map/dot_general | solution.py:46
  42.2 5.6 %fusion.11 = bf16[16,1536]{1,0:T(8,128)(2,1)S(1)} fusion(f32[1600,1536]{1,0:T(8,128)S(1)} %fusion.58, f32[1536]{0:T(1024)S(1)} %copy-done.6, f32[1536]{0:T(1024)S(1)} %copy-done.7, s32[1600]{0:T(1024)S(1)} %add_select_fusion.8), kind=kOutput, calls=%fused_computation.16 | convolution fusion | flops 486679552 | bytes 9898240 | tf_op jit(solution)/shard_map/dot_general | solution.py:50
  47.9 10.2 %all_gather.3 = bf16[64,1536]{1,0:T(8,128)(2,1)S(1)} all-gather(bf16[16,1536]{1,0:T(8,128)(2,1)S(1)} %fusion.11), channel_id=1, replica_groups=mesh['dp'=8,'leaf'=4] {'leaf'}, dimensions={0}, use_global_device_ids=true | all-gather | bytes 245760 | tf_op jit(solution)/shard_map/all_gather | solution.py:52
  58.0 1.8 fusion.59
  59.8 1.9 reshape.411
  62.3 1.5 select_reduce_fusion
  64.6 1.1 tile.13
  65.7 2.3 %fusion.15 = pred[64,64]{1,0:T(8,128)(4,1)S(1)} fusion(s32[64,48]{1,0:T(8,128)} %add_select_fusion, pred[64,48]{1,0:T(8,128)(4,1)S(1)} %slice.67), kind=kLoop, calls=%fused_computation.21 | loop fusion | flops 585728 | bytes 19456 | tf_op jit(solution)/shard_map/reduce_or | solution.py:31
  69.5 1.8 tile.15
  71.3 2.4 %fusion.20 = f32[64,1536]{1,0:T(8,128)} fusion(bf16[1024,1536]{1,0:T(8,128)(2,1)S(1)} %copy-done, bf16[64,1024]{1,0:T(8,128)(2,1)S(1)} %tile.13, bf16[64,1024]{1,0:T(8,128)(2,1)} %tile.15, s32[1024]{0:T(1024)} %add_select_fusion.9, s32[64]{0:T(128)} %reduce.3, s32[64]{0:T(128)} %reduce), kind=kOutput, calls=%fused_computation.33 | convolution fusion | flops 201654272 | bytes 3805696 | tf_op jit(solution)/shard_map/dot_general | solution.py:73
  73.9 24.6 %reduce-scatter.5.cloned.1.call-done = f32[16,1536]{1,0:T(8,128)} async-done(((f32[64,1536]{1,0:T(8,128)}), f32[16,1536]{1,0:T(8,128)}) %reduce-scatter.5.cloned.1.call-update) | async-done | bytes 98320 | tf_op jit(solution)/shard_map/reduce_scatter | solution.py:74
  98.6 10.8 %multiply_reduce_fusion = (f32[1536]{0:T(1024)S(1)}, f32[1536]{0:T(1024)S(1)}, f32[1600,1536]{1,0:T(8,128)S(1)}) fusion(f32[1600,1536]{1,0:T(8,128)} %copy-done.2, f32[1536]{0:T(1024)} %param.10, f32[1536]{0:T(1024)} %param.9, f32[16,1536]{1,0:T(8,128)} %reduce-scatter.5.cloned.1.call-done, s32[1600]{0:T(1024)} %copy-done.5), kind=kOutput, calls=%fused_computation.1 | convolution fusion | flops 503855104 | bytes 19790080 | tf_op jit(solution)/shard_map/dot_general | solution.py:100
  109.5 2.4 %fusion.7 = f32[384,1536]{1,0:T(8,128)S(1)} fusion(bf16[1600,384]{1,0:T(8,128)(2,1)S(1)} %copy-done.3, f32[1600,1536]{1,0:T(8,128)S(1)} %get-tuple-element.46, f32[1536]{0:T(1024)S(1)} %copy-done.8), kind=kOutput, calls=%fused_computation.13 | convolution fusion | flops 1892352000 | bytes 13424640 | tf_op jit(solution)/shard_map/dot_general | solution.py:105
  111.9 1.6 pad_maximum_fusion
  113.6 3.4 %copy.27 = f32[386,1536]{0,1:T(8,128)} copy(f32[386,1536]{1,0:T(8,128)} %pad_maximum_fusion) | data formatting | bytes 4743168
  117.0 0.9 reshape.412
  117.9 1.0 copy.36
  120.0 4.6 %all-to-all-start = ((bf16[8,64,322]{2,1,0:T(8,128)(2,1)}), bf16[8,64,322]{2,1,0:T(8,128)(2,1)}, u32[]{:S(2)}, u32[]{:S(2)}) async-start(bf16[8,64,322]{2,1,0:T(8,128)(2,1)} %pad_maximum_fusion.1), calls=%async_computation.1 | async-start | bytes 786432 | tf_op jit(solution)/shard_map/all_to_all | solution.py:89
  124.6 19.1 %all-to-all-done = bf16[8,64,322]{2,1,0:T(8,128)(2,1)} async-done(((bf16[8,64,322]{2,1,0:T(8,128)(2,1)}), bf16[8,64,322]{2,1,0:T(8,128)(2,1)}, u32[]{:S(2)}, u32[]{:S(2)}) %all-to-all-start) | async-done | bytes 329760 | tf_op jit(solution)/shard_map/all_to_all | solution.py:89
  143.7 1.1 slice.71
  145.7 1.1 copy.34
  146.7 1.1 copy.33
  148.6 1.0 copy.32
  149.7 14.1 %reduce-scatter.7.cloned.1.call-done = f32[192,386]{1,0:T(8,128)} async-done(((f32[1536,386]{1,0:T(8,128)}), f32[192,386]{1,0:T(8,128)}) %reduce-scatter.7.cloned.1.call-update) | async-done | bytes 296464
  163.8 1.9 copy.28
  166.3 1.0 slice.76
  167.3 1.4 fusion.60
  168.7 42.4 %all-reduce.2.cloned.1.call-done = f32[386,192]{1,0:T(8,128)} async-done(((f32[386,192]{1,0:T(8,128)}), f32[386,192]{1,0:T(8,128)}) %all-reduce.2.cloned.1.call-update) | async-done | bytes 296464 | tf_op jit(solution)/shard_map/psum | solution.py:111
  211.1 1.0 slice.68
  213.0 1.3 fusion.56
  (56 shorter events, 12.4 us)
Async XLA Ops:
  7.2 50.9 %copy-start = (bf16[1024,1536]{1,0:T(8,128)(2,1)S(1)}, bf16[1024,1536]{1,0:T(8,128)(2,1)}, u32[]{:S(2)}) copy-start(bf16[1024,1536]{1,0:T(8,128)(2,1)} %param.11) | copy-start | bytes 9437188
  7.2 3.2 %copy-start.1 = (s32[64]{0:T(128)S(1)}, s32[64]{0:T(128)}, u32[]{:S(2)}) copy-start(s32[64]{0:T(128)} %param.12) | copy-start | bytes 772
  7.2 91.4 %reduce-scatter.5.cloned.1.call-start = ((), (), s32[]{:S(2)}) async-start(), calls=%async_computation.3 | async-start | bytes 491520 | tf_op jit(solution)/shard_map/reduce_scatter | solution.py:74
  7.3 34.9 %copy-start.5 = (s32[1600]{0:T(1024)}, s32[1600]{0:T(1024)S(1)}, u32[]{:S(2)}) copy-start(s32[1600]{0:T(1024)S(1)} %add_select_fusion.8) | copy-start | bytes 19204
  35.1 7.1 %copy-start.6 = (f32[1536]{0:T(1024)S(1)}, f32[1536]{0:T(1024)}, u32[]{:S(2)}) copy-start(f32[1536]{0:T(1024)} %param.10) | copy-start | bytes 18436
  35.1 7.1 %copy-start.7 = (f32[1536]{0:T(1024)S(1)}, f32[1536]{0:T(1024)}, u32[]{:S(2)}) copy-start(f32[1536]{0:T(1024)} %param.9) | copy-start | bytes 18436
  42.2 5.7 %copy-start.2 = (f32[1600,1536]{1,0:T(8,128)}, f32[1600,1536]{1,0:T(8,128)S(1)}, u32[]{:S(2)}) copy-start(f32[1600,1536]{1,0:T(8,128)S(1)} %fusion.58) | copy-start | bytes 29491204
  73.7 35.8 %copy-start.8 = (f32[1536]{0:T(1024)S(1)}, f32[1536]{0:T(1024)}, u32[]{:S(2)}) copy-start(f32[1536]{0:T(1024)} %param.9) | copy-start | bytes 18436
  73.7 90.1 %reduce-scatter.7.cloned.1.call-start = ((), (), s32[]{:S(2)}) async-start(), calls=%async_computation.5 | async-start | bytes 3538944
  98.6 10.9 %copy-start.3 = (bf16[1600,384]{1,0:T(8,128)(2,1)S(1)}, bf16[1600,384]{1,0:T(8,128)(2,1)}, u32[]{:S(2)}) copy-start(bf16[1600,384]{1,0:T(8,128)(2,1)} %param.7) | copy-start | bytes 3686404
  111.9 7.0 %copy-start.4 = (bf16[64,1]{1,0:T(8,128)(2,1)S(1)}, bf16[64,1]{1,0:T(8,128)(2,1)}, u32[]{:S(2)}) copy-start(bf16[64,1]{1,0:T(8,128)(2,1)} %get-tuple-element.42) | copy-start | bytes 388
  120.0 23.8 %all-to-all-start = ((bf16[8,64,322]{2,1,0:T(8,128)(2,1)}), bf16[8,64,322]{2,1,0:T(8,128)(2,1)}, u32[]{:S(2)}, u32[]{:S(2)}) async-start(bf16[8,64,322]{2,1,0:T(8,128)(2,1)} %pad_maximum_fusion.1), calls=%async_computation.1 | async-start | bytes 786432 | tf_op jit(solution)/shard_map/all_to_all | solution.py:89
  124.6 86.6 %all-reduce.2.cloned.1.call-start = ((), (), s32[]{:S(2)}) async-start(), calls=%async_computation.4 | async-start | bytes 802816 | tf_op jit(solution)/shard_map/psum | solution.py:111
Sparse Core Ops, SparseCore 0:
  73.8 24.7 reduce-scatter.4
  117.1 46.6 reduce-scatter.6
  166.8 44.2 all-reduce.1
where the time goes:
time: 222 us; the launch traced here: 221 us
  waiting for transfers between devices  100 us (45%)
  local copies, waits for them, and re-layouts  47.8 us (22%)
  matrix products  28.8 us (13%)
  other arithmetic  14.8 us (7%)
  between operations  14 us (6%)
  blocking collectives  10.2 us (5%)
  starting transfers between devices  4.89 us (2%)
    psum x1, waiting for transfers between devices, shards(): lax.psum(lax.psum_scatter(stacked, 'dp', scatter_dimension=1, tiled=True)...  42.4 us
    gather x2, local copies, waits for them, and re-layouts, shards(): block_of = subtree_map[safe_ids // SUB_SIZE]  24.8 us
    reduce_scatter x1, waiting for transfers between devices, shards(): lax.psum_scatter(grad_part, 'leaf', scatter_dimension=0, tiled=True)  24.6 us
    all_to_all x1, waiting for transfers between devices, shards(): recv = lax.all_to_all(send, 'dp', split_axis=0, concat_axis=0, tiled=True)  19.1 us
    unnamed x4, waiting for transfers between devices  14.2 us
    dot_general x1, matrix products, shards(): jnp.dot(select.T, emb_grad / P_SIZE, precision=HIGHEST, preferred_element...  10.8 us
    all_gather x1, blocking collectives, shards(): grouped = lax.all_gather(embedded, 'leaf', axis=0, tiled=True)  10.2 us
    unnamed x25, local copies, waits for them, and re-layouts  9.45 us
  transfers between devices with their start and end apart: 4, of which 4 were waited for; matrix products, arithmetic and copies ran while one was open for 5% of the time, Pallas kernels for 0%

commit v1 on v0

--- a/solution.py
+++ b/solution.py
@@ -108,7 +108,10 @@
     gain_term = jnp.sum(pixel_gradient * linear_scores, axis=0)
     shift_term = jnp.sum(pixel_gradient, axis=0)
     stacked = jnp.concatenate([head_term, gain_term[None], shift_term[None]], axis=0)
-    reduced = lax.psum(lax.psum_scatter(stacked, "dp", scatter_dimension=1, tiled=True), "leaf")
+    reduced = jnp.sum(
+        lax.all_gather(lax.psum_scatter(stacked, "dp", scatter_dimension=1, tiled=True), "leaf"),
+        axis=0,
+    )
     e_size = head_term.shape[0]
     return (reduced[:e_size], reduced[e_size], reduced[e_size + 1], node_grad)
 

time: 222 us -> 202 us (0.910)
  waiting for transfers between devices: 100 us -> 76.9 us
  local copies, waits for them, and re-layouts: 47.8 us -> 51.2 us
    psum x1 -> x0, waiting for transfers between devices: 42.4 us -> none  [shards(): lax.psum(lax.psum_scatter(stacked, 'dp', scatter_dimension=1, tiled=True)...]
    unnamed x4, waiting for transfers between devices: 14.2 us -> 37.9 us
    all_to_all x1, waiting for transfers between devices: 19.1 us -> 12.5 us  [shards(): recv = lax.all_to_all(send, 'dp', split_axis=0, concat_axis=0, tiled=True)]
    unnamed x25 -> x29, local copies, waits for them, and re-layouts: 9.45 us -> 13 us
  transfers between devices with their start and end apart: 4 -> 4, of which waited for: 4 -> 4; matrix products, arithmetic and copies ran while one was open for 5% -> 7% of each run, Pallas kernels for 0% -> 0%
where the time goes in v1:
time: 202 us; the launch traced here: 201 us
  waiting for transfers between devices  76.9 us (38%)
  local copies, waits for them, and re-layouts  51.2 us (25%)
  matrix products  28.8 us (14%)
  other arithmetic  15.4 us (8%)
  between operations  14.1 us (7%)
  blocking collectives  10.2 us (5%)
  starting transfers between devices  4.4 us (2%)
    unnamed x4, waiting for transfers between devices  37.9 us
    gather x2, local copies, waits for them, and re-layouts, shards(): block_of = subtree_map[safe_ids // SUB_SIZE]  24.8 us
    reduce_scatter x1, waiting for transfers between devices, shards(): lax.psum_scatter(grad_part, 'leaf', scatter_dimension=0, tiled=True)  24.7 us
    unnamed x29, local copies, waits for them, and re-layouts  13 us
    all_to_all x1, waiting for transfers between devices, shards(): recv = lax.all_to_all(send, 'dp', split_axis=0, concat_axis=0, tiled=True)  12.5 us
    dot_general x1, matrix products, shards(): jnp.dot(select.T, emb_grad / P_SIZE, precision=HIGHEST, preferred_element...  10.8 us
    all_gather x1, blocking collectives, shards(): grouped = lax.all_gather(embedded, 'leaf', axis=0, tiled=True)  10.2 us
    dot_general x1, matrix products, shards(): jnp.dot(select, active, precision=HIGHEST, preferred_element_type=jnp.flo...  5.64 us
  transfers between devices with their start and end apart: 4, of which 4 were waited for; matrix products, arithmetic and copies ran while one was open for 7% of the time, Pallas kernels for 0%

profile of v1, /device:TPU:0, one launch (start us, length us, event | category | flops | bytes accessed | tf_op | source)
XLA Modules:
  0.0 200.9 jit_solution(15265964793717982472)
XLA Ops:
  9.2 24.7 %gather_fusion = s32[4096]{0:T(1024)S(1)} fusion(s32[64]{0:T(128)S(1)} %copy-done.1, s32[4096]{0:T(1024)S(1)} %broadcast_clamp_fusion), kind=kCustom, calls=%fused_computation | custom fusion | bytes 49152 | tf_op jit(solution)/shard_map/gather | solution.py:56
  36.2 4.3 %fusion.58 = f32[1600,1536]{1,0:T(8,128)S(1)} fusion(bf16[1600,384]{1,0:T(8,128)(2,1)} %param.7, bf16[384,1536]{1,0:T(8,128)(2,1)} %param.8), kind=kOutput, calls=%fused_computation.131 | convolution fusion | flops 1887436800 | bytes 12238848 | tf_op jit(solution)/shard_map/dot_general | solution.py:46
  40.6 5.6 %fusion.11 = bf16[16,1536]{1,0:T(8,128)(2,1)S(1)} fusion(f32[1600,1536]{1,0:T(8,128)S(1)} %fusion.58, f32[1536]{0:T(1024)S(1)} %copy-done.7, f32[1536]{0:T(1024)S(1)} %copy-done.8, s32[1600]{0:T(1024)S(1)} %add_select_fusion.8), kind=kOutput, calls=%fused_computation.16 | convolution fusion | flops 486679552 | bytes 9898240 | tf_op jit(solution)/shard_map/dot_general | solution.py:50
  46.2 10.2 %all_gather.9 = bf16[64,1536]{1,0:T(8,128)(2,1)S(1)} all-gather(bf16[16,1536]{1,0:T(8,128)(2,1)S(1)} %fusion.11), channel_id=1, replica_groups=mesh['dp'=8,'leaf'=4] {'leaf'}, dimensions={0}, use_global_device_ids=true | all-gather | bytes 245760 | tf_op jit(solution)/shard_map/all_gather | solution.py:52
  56.4 1.8 fusion.59
  58.2 1.9 reshape.411
  60.7 1.5 select_reduce_fusion
  63.6 1.1 tile.13
  64.7 1.1 fusion.15
  67.9 1.8 tile.15
  69.7 2.4 %fusion.20 = f32[64,1536]{1,0:T(8,128)} fusion(bf16[1024,1536]{1,0:T(8,128)(2,1)S(1)} %copy-done, bf16[64,1024]{1,0:T(8,128)(2,1)S(1)} %tile.13, bf16[64,1024]{1,0:T(8,128)(2,1)} %tile.15, s32[1024]{0:T(1024)S(1)} %add_select_fusion.9, s32[64]{0:T(128)S(1)} %reduce.4, s32[64]{0:T(128)} %reduce.1), kind=kOutput, calls=%fused_computation.33 | convolution fusion | flops 201654272 | bytes 3805696 | tf_op jit(solution)/shard_map/dot_general | solution.py:73
  72.4 24.7 %reduce-scatter.5.cloned.1.call-done = f32[16,1536]{1,0:T(8,128)} async-done(((f32[64,1536]{1,0:T(8,128)}), f32[16,1536]{1,0:T(8,128)}) %reduce-scatter.5.cloned.1.call-update) | async-done | bytes 98320 | tf_op jit(solution)/shard_map/reduce_scatter | solution.py:74
  97.0 10.8 %multiply_reduce_fusion = (f32[1536]{0:T(1024)S(1)}, f32[1536]{0:T(1024)S(1)}, f32[1600,1536]{1,0:T(8,128)S(1)}) fusion(f32[1600,1536]{1,0:T(8,128)} %copy-done.2, f32[1536]{0:T(1024)} %param.10, f32[1536]{0:T(1024)} %param.9, f32[16,1536]{1,0:T(8,128)} %reduce-scatter.5.cloned.1.call-done, s32[1600]{0:T(1024)} %copy-done.6), kind=kOutput, calls=%fused_computation.1 | convolution fusion | flops 503855104 | bytes 19790080 | tf_op jit(solution)/shard_map/dot_general | solution.py:100
  107.9 2.4 %fusion.7 = f32[384,1536]{1,0:T(8,128)S(1)} fusion(bf16[1600,384]{1,0:T(8,128)(2,1)S(1)} %copy-done.3, f32[1600,1536]{1,0:T(8,128)S(1)} %get-tuple-element.34, f32[1536]{0:T(1024)S(1)} %copy-done.9), kind=kOutput, calls=%fused_computation.13 | convolution fusion | flops 1892352000 | bytes 13424640 | tf_op jit(solution)/shard_map/dot_general | solution.py:105
  110.4 1.6 pad_maximum_fusion
  112.0 3.4 %copy.28 = f32[386,1536]{0,1:T(8,128)} copy(f32[386,1536]{1,0:T(8,128)} %pad_maximum_fusion) | data formatting | bytes 4743168
  116.4 1.7 copy.41
  118.1 37.8 %reduce-scatter.7.cloned.1.call-done = f32[192,386]{1,0:T(8,128)} async-done(((f32[1536,386]{1,0:T(8,128)}), f32[192,386]{1,0:T(8,128)}) %reduce-scatter.7.cloned.1.call-update) | async-done | bytes 296464
  156.0 1.2 copy.29
  159.0 1.9 pad_maximum_fusion.1
  160.8 4.1 %all-to-all-start = ((bf16[8,64,322]{2,1,0:T(8,128)(2,1)}), bf16[8,64,322]{2,1,0:T(8,128)(2,1)}, u32[]{:S(2)}, u32[]{:S(2)}) async-start(bf16[8,64,322]{2,1,0:T(8,128)(2,1)} %pad_maximum_fusion.1), calls=%async_computation.1 | async-start | bytes 786432 | tf_op jit(solution)/shard_map/all_to_all | solution.py:89
  164.9 12.5 %all-to-all-done = bf16[8,64,322]{2,1,0:T(8,128)(2,1)} async-done(((bf16[8,64,322]{2,1,0:T(8,128)(2,1)}), bf16[8,64,322]{2,1,0:T(8,128)(2,1)}, u32[]{:S(2)}, u32[]{:S(2)}) %all-to-all-start) | async-done | bytes 329760 | tf_op jit(solution)/shard_map/all_to_all | solution.py:89
  177.5 1.1 slice.71
  179.4 1.1 copy.39
  180.5 1.1 copy.38
  182.3 1.0 copy.37
  183.4 1.0 slice.76
  185.0 1.4 fusion.60
  186.4 1.8 all-gather.4.cloned.1.call-done
  188.2 1.6 reduce_sum.49
  191.3 1.5 copy.32
  192.8 1.5 copy.33
  (61 shorter events, 15.2 us)
Async XLA Ops:
  7.2 49.3 %copy-start = (bf16[1024,1536]{1,0:T(8,128)(2,1)S(1)}, bf16[1024,1536]{1,0:T(8,128)(2,1)}, u32[]{:S(2)}) copy-start(bf16[1024,1536]{1,0:T(8,128)(2,1)} %param.11) | copy-start | bytes 9437188
  7.2 2.0 copy-start.1
  7.2 89.8 %reduce-scatter.5.cloned.1.call-start = ((), (), s32[]{:S(2)}) async-start(), calls=%async_computation.3 | async-start | bytes 491520 | tf_op jit(solution)/shard_map/reduce_scatter | solution.py:74
  7.3 33.3 %copy-start.6 = (s32[1600]{0:T(1024)}, s32[1600]{0:T(1024)S(1)}, u32[]{:S(2)}) copy-start(s32[1600]{0:T(1024)S(1)} %add_select_fusion.8) | copy-start | bytes 19204
  33.9 6.7 %copy-start.7 = (f32[1536]{0:T(1024)S(1)}, f32[1536]{0:T(1024)}, u32[]{:S(2)}) copy-start(f32[1536]{0:T(1024)} %param.10) | copy-start | bytes 18436
  33.9 6.7 %copy-start.8 = (f32[1536]{0:T(1024)S(1)}, f32[1536]{0:T(1024)}, u32[]{:S(2)}) copy-start(f32[1536]{0:T(1024)} %param.9) | copy-start | bytes 18436
  40.6 5.7 %copy-start.2 = (f32[1600,1536]{1,0:T(8,128)}, f32[1600,1536]{1,0:T(8,128)S(1)}, u32[]{:S(2)}) copy-start(f32[1600,1536]{1,0:T(8,128)S(1)} %fusion.58) | copy-start | bytes 29491204
  62.2 0.6 copy-start.4
  66.6 0.6 copy-start.5
  72.1 35.8 %copy-start.9 = (f32[1536]{0:T(1024)S(1)}, f32[1536]{0:T(1024)}, u32[]{:S(2)}) copy-start(f32[1536]{0:T(1024)} %param.9) | copy-start | bytes 18436
  72.1 83.8 %reduce-scatter.7.cloned.1.call-start = ((), (), s32[]{:S(2)}) async-start(), calls=%async_computation.5 | async-start | bytes 3538944
  97.0 10.9 %copy-start.3 = (bf16[1600,384]{1,0:T(8,128)(2,1)S(1)}, bf16[1600,384]{1,0:T(8,128)(2,1)}, u32[]{:S(2)}) copy-start(bf16[1600,384]{1,0:T(8,128)(2,1)} %param.7) | copy-start | bytes 3686404
  115.5 72.7 %all-gather.4.cloned.1.call-start = ((), (), s32[]{:S(2)}) async-start(), calls=%async_computation.4 | async-start | bytes 1966080 | tf_op jit(solution)/shard_map/all_gather | solution.py:112
  160.8 16.7 %all-to-all-start = ((bf16[8,64,322]{2,1,0:T(8,128)(2,1)}), bf16[8,64,322]{2,1,0:T(8,128)(2,1)}, u32[]{:S(2)}, u32[]{:S(2)}) async-start(bf16[8,64,322]{2,1,0:T(8,128)(2,1)} %pad_maximum_fusion.1), calls=%async_computation.1 | async-start | bytes 786432 | tf_op jit(solution)/shard_map/all_to_all | solution.py:89
Sparse Core Ops, SparseCore 0:
  72.2 24.7 reduce-scatter.4
  115.6 40.3 reduce-scatter.6
  158.2 29.9 all-gather.3
